TPU v7x, 256 devices: a whole 4x4x8 slice. The times are simulated.
256 devices in a mesh: dp: 16 (over z_lo, x), tensor: 16 (over z_hi, y, core).
Axes of the slice: x: 4, y: 4, z: 8 (z_hi: 2, z_lo: 4; z = z_hi * 4 + z_lo), core: 2. Of those that a mesh axis runs over, the one named last changes fastest.
Arguments:
- cotangent: bfloat16 [8192, 4096], P(('dp', 'tensor')), may hold values from -6 to 6
- gate: bfloat16 [8192, 14336], P('dp', 'tensor'), may hold values from -8 to 8
- up: bfloat16 [8192, 14336], P('dp', 'tensor'), may hold values from -6 to 6
- w_down: bfloat16 [4, 14336, 4096], P(None, 'tensor', 'dp'), may hold values from -0.03125 to 0.03125
- language: int32 [16], replicated, may hold values from 0 to 3
Outputs:
- d_gate: bfloat16 [8192, 14336], P('dp', 'tensor')
- d_up: bfloat16 [8192, 14336], P('dp', 'tensor')
- d_weight: float32 [4, 14336, 4096], P(None, 'tensor', 'dp')
All inputs are finite; a program needn't handle non-finite values.
Results may differ from a plain program's by a relative error of at most 0.0029.
Values may be sent and summed in bfloat16 or wider, within the bound.
No kernel may reach another device: no remote copies, remote signals or barrier semaphores. Data moves between devices by JAX's collectives and lax.ppermute only.
A program may use at most 128 MiB of HBM per device.

v0:
```python
import jax
import jax.numpy as jnp
from jax import lax
from jax.sharding import PartitionSpec as P


def shards(cotangent, gate, up, w_down, language):
    groups = lax.axis_size("dp")
    variants = w_down.shape[0]
    ff_dev = w_down.shape[1]
    feat_dev = w_down.shape[2]
    out_rows = lax.all_gather(cotangent, "tensor", axis=0, tiled=True)
    gate_f = gate.astype(jnp.float32)
    up_f = up.astype(jnp.float32)
    sig = jax.nn.sigmoid(gate_f)
    act = gate_f * sig
    hidden = (act * up_f).astype(jnp.bfloat16)
    slabs = jnp.take(w_down, language, axis=0)
    received = lax.all_to_all(slabs, "dp", split_axis=0, concat_axis=2, tiled=True)
    weights = received[0]
    d_hidden = lax.dot_general(
        out_rows, weights, (((1,), (1,)), ((), ())), preferred_element_type=jnp.float32
    )
    d_up = (d_hidden * act).astype(jnp.bfloat16)
    d_gate = (d_hidden * up_f * sig * (1.0 + gate_f * (1.0 - sig))).astype(jnp.bfloat16)
    selector = (language[None, :] == jnp.arange(variants, dtype=jnp.int32)[:, None]).astype(
        jnp.float32
    )
    partial_term = lax.dot_general(
        hidden, out_rows, (((0,), (0,)), ((), ())), preferred_element_type=jnp.float32
    )
    pieces = lax.all_to_all(
        partial_term.reshape(ff_dev, groups, feat_dev),
        "dp",
        split_axis=1,
        concat_axis=1,
        tiled=True,
    )
    d_weight = jnp.einsum("lg,fgd->lfd", selector, pieces, precision=lax.Precision.HIGHEST)
    return (d_gate, d_up, d_weight)


def solution(mesh):
    return jax.shard_map(
        shards,
        mesh=mesh,
        in_specs=(
            P(("dp", "tensor"), None),
            P("dp", "tensor"),
            P("dp", "tensor"),
            P(None, "tensor", "dp"),
            P(),
        ),
        out_specs=(P("dp", "tensor"), P("dp", "tensor"), P(None, "tensor", "dp")),
        check_vma=False,
    )
```

profile of v0, /device:TPU:64, one launch (start us, length us, event | category | flops | bytes accessed | tf_op | source)
XLA Modules:
  0.0 566.6 jit_solution(13106661074899269644)
XLA Ops:
  7.2 0.0 copy-start
  7.2 0.8 compare_and_fusion
  8.0 0.7 compare_select_fusion
  8.6 0.0 copy-done
  8.7 4.0 gather_fusion
  12.7 6.9 %broadcast_select_fusion = bf16[16,896,256]{2,1,0:T(8,128)(2,1)} fusion(bf16[16,896,256]{2,1,0:T(8,128)(2,1)} %gather_fusion, pred[16]{0:T(512)(128)(4,1)S(1)} %compare_and_fusion), kind=kLoop, calls=%fused_computation.4 | loop fusion | flops 3670016 | bytes 14680080 | tf_op jit(solution)/shard_map/jit(_take)/select_n | solution.py:18
  19.6 0.0 copy-start.2
  19.6 0.0 copy-start.3
  19.6 8.2 %all-to-all-start = ((bf16[16,896,256]{2,1,0:T(8,128)(2,1)}), bf16[16,896,256]{2,1,0:T(8,128)(2,1)}, u32[]{:S(2)}, u32[]{:S(2)}) async-start(bf16[16,896,256]{2,1,0:T(8,128)(2,1)} %broadcast_select_fusion), calls=%async_computation | async-start | bytes 14680064 | tf_op jit(solution)/shard_map/all_to_all | solution.py:19
  27.7 0.0 all-gather.2.cloned.1.call-start
  27.8 0.7 all-gather.2.cloned.1.call-update
  28.5 0.0 copy-done.2
  28.5 0.5 copy.26
  29.0 0.0 copy-done.3
  29.0 0.5 copy.25
  29.6 121.4 %all-gather.2.cloned.1.call-done = bf16[512,4096]{1,0:T(8,128)(2,1)} async-done(((bf16[32,4096]{1,0:T(8,128)(2,1)}), bf16[512,4096]{1,0:T(8,128)(2,1)}) %all-gather.2.cloned.1.call-update) | async-done | bytes 4194320 | tf_op jit(solution)/shard_map/all_gather | solution.py:12
  150.9 9.5 %fusion.11 = f32[896,4096]{1,0:T(8,128)} fusion(bf16[512,4096]{1,0:T(8,128)(2,1)} %all-gather.2.cloned.1.call-done, bf16[512,896]{0,1:T(8,128)(2,1)S(1)} %copy.25, bf16[512,896]{0,1:T(8,128)(2,1)S(1)} %copy.26), kind=kOutput, calls=%fused_computation.20 | convolution fusion | flops 3761766400 | bytes 20709376 | tf_op jit(solution)/shard_map/dot_general | solution.py:29
  160.4 12.0 %copy.36 = f32[112,16,8,256]{3,2,0,1:T(8,128)} copy(f32[112,16,8,256]{3,2,1,0:T(8,128)} %bitcast.20) | data formatting | bytes 29360128 | tf_op jit(solution)/shard_map/reshape | solution.py:33
  172.4 44.2 %all-to-all-done = bf16[16,896,256]{2,1,0:T(8,128)(2,1)} async-done(((bf16[16,896,256]{2,1,0:T(8,128)(2,1)}), bf16[16,896,256]{2,1,0:T(8,128)(2,1)}, u32[]{:S(2)}, u32[]{:S(2)}) %all-to-all-start) | async-done | bytes 7340064 | tf_op jit(solution)/shard_map/all_to_all | solution.py:19
  216.6 5.2 all-to-all-start.1
  221.7 11.1 %copy.24 = bf16[1,896,16,256]{1,3,2,0:T(8,128)(2,1)} copy(bf16[1,896,16,256]{3,1,2,0:T(8,128)(2,1)} %bitcast.1) | data formatting | bytes 14680064 | tf_op jit(solution)/shard_map/all_to_all | solution.py:19
  232.9 9.8 %fusion.10 = (bf16[512,896]{0,1:T(8,128)(2,1)}, bf16[512,896]{0,1:T(8,128)(2,1)S(1)}) fusion(bf16[512,896]{0,1:T(8,128)(2,1)S(1)} %copy.26, bf16[512,896]{0,1:T(8,128)(2,1)S(1)} %copy.25, bf16[896,4096]{0,1:T(8,128)(2,1)} %bitcast.21, bf16[512,4096]{1,0:T(8,128)(2,1)} %all-gather.2.cloned.1.call-done), kind=kOutput, calls=%fused_computation.19 | convolution fusion | flops 3764977664 | bytes 15204352 | tf_op jit(solution)/shard_map/dot_general | solution.py:21
  242.7 0.0 copy-start.4
  242.7 2.2 copy.30
  244.9 1.3 copy.29
  246.2 292.8 %all-to-all-done.1 = f32[896,16,256]{2,0,1:T(8,128)} async-done(((f32[896,16,256]{2,0,1:T(8,128)}), f32[896,16,256]{2,0,1:T(8,128)}, u32[]{:S(2)}, u32[]{:S(2)}) %all-to-all-start.1) | async-done | bytes 14680096 | tf_op jit(solution)/shard_map/all_to_all | solution.py:32
  539.0 0.0 copy-done.4
  539.0 0.0 copy-start.1
  539.0 18.3 %fusion = f32[4,896,256]{2,0,1:T(4,128)S(1)} fusion(f32[896,16,256]{2,0,1:T(8,128)} %all-to-all-done.1, s32[16]{0:T(128)S(1)} %copy-done.4), kind=kOutput, calls=%fused_computation.2 | convolution fusion | flops 176160832 | bytes 18350144 | tf_op jit(solution)/shard_map/lg,fgd->lfd/dot_general | solution.py:39
  557.3 2.5 copy.31
  559.8 0.0 copy-done.1
  (1 shorter events, 0.0 us)
Async XLA Ops:
  7.2 1.5 copy-start
  19.6 8.9 %copy-start.2 = (bf16[512,896]{1,0:T(8,128)(2,1)S(1)}, bf16[512,896]{1,0:T(8,128)(2,1)}, u32[]{:S(2)}) copy-start(bf16[512,896]{1,0:T(8,128)(2,1)} %param.6) | copy-start | bytes 2752516
  19.6 9.4 %copy-start.3 = (bf16[512,896]{1,0:T(8,128)(2,1)S(1)}, bf16[512,896]{1,0:T(8,128)(2,1)}, u32[]{:S(2)}) copy-start(bf16[512,896]{1,0:T(8,128)(2,1)} %param.7) | copy-start | bytes 2752516
  19.6 197.0 %all-to-all-start = ((bf16[16,896,256]{2,1,0:T(8,128)(2,1)}), bf16[16,896,256]{2,1,0:T(8,128)(2,1)}, u32[]{:S(2)}, u32[]{:S(2)}) async-start(bf16[16,896,256]{2,1,0:T(8,128)(2,1)} %broadcast_select_fusion), calls=%async_computation | async-start | bytes 14680064 | tf_op jit(solution)/shard_map/all_to_all | solution.py:19
  27.7 123.2 %all-gather.2.cloned.1.call-start = ((), (), s32[]{:S(2)}) async-start(), calls=%async_computation.2 | async-start | bytes 4456448 | tf_op jit(solution)/shard_map/all_gather | solution.py:12
  216.6 322.4 %all-to-all-start.1 = ((f32[896,16,256]{2,0,1:T(8,128)}), f32[896,16,256]{2,0,1:T(8,128)}, u32[]{:S(2)}, u32[]{:S(2)}) async-start(f32[896,16,256]{2,0,1:T(8,128)} %bitcast.19), calls=%async_computation.1 | async-start | bytes 29360128 | tf_op jit(solution)/shard_map/all_to_all | solution.py:32
  242.7 296.3 %copy-start.4 = (s32[16]{0:T(128)S(1)}, s32[16]{0:T(128)}, u32[]{:S(2)}) copy-start(s32[16]{0:T(128)} %param.9) | copy-start | bytes 196
  539.0 20.8 %copy-start.1 = (bf16[4,896,256]{2,1,0:T(8,128)(2,1)S(1)}, bf16[4,896,256]{2,1,0:T(8,128)(2,1)}, u32[]{:S(2)}) copy-start(bf16[4,896,256]{2,1,0:T(8,128)(2,1)} %param.8) | copy-start | bytes 5505028
Sparse Core Ops, SparseCore 0:
  31.3 119.5 all-gather.1
where the time goes:
time: 567 us
  waiting for transfers between devices  459 us (81%)
  matrix products  37.6 us (7%)
  local copies, waits for them, and re-layouts  34.2 us (6%)
  between operations  14.1 us (2%)
  starting transfers between devices  13.4 us (2%)
  other arithmetic  8.33 us (1%)
    all_to_all x1, waiting for transfers between devices, shards(): lax.all_to_all(partial_term.reshape(ff_dev, groups, feat_dev), 'dp', spli...  293 us
    all_gather x1, waiting for transfers between devices, shards(): out_rows = lax.all_gather(cotangent, 'tensor', axis=0, tiled=True)  121 us
    all_to_all x1, waiting for transfers between devices, shards(): lax.all_to_all(slabs, 'dp', split_axis=0, concat_axis=2, tiled=True)  44.2 us
    dot_general x1, matrix products, shards(): jnp.einsum('lg,fgd->lfd', selector, pieces, precision=lax.Precision.HIGHEST)  18.3 us
    reshape x1, local copies, waits for them, and re-layouts, shards(): partial_term.reshape(ff_dev, groups, feat_dev)  12 us
  transfers between devices with their start and end apart: 3, of which 3 were waited for; matrix products, arithmetic and copies ran while one was open for 8% of the time, Pallas kernels for 0%

commit v1 on v0

--- a/solution.py
+++ b/solution.py
@@ -29,12 +29,18 @@
     partial_term = lax.dot_general(
         hidden, out_rows, (((0,), (0,)), ((), ())), preferred_element_type=jnp.float32
     )
-    pieces = lax.all_to_all(
-        partial_term.reshape(ff_dev, groups, feat_dev),
-        "dp",
-        split_axis=1,
-        concat_axis=1,
-        tiled=True,
+    pieces = jnp.concatenate(
+        lax.all_to_all(
+            jnp.stack(
+                jnp.split(
+                    partial_term.reshape(ff_dev, groups, feat_dev), lax.axis_size("dp"), axis=1
+                )
+            ),
+            "dp",
+            0,
+            0,
+        ),
+        axis=1,
     )
     d_weight = jnp.einsum("lg,fgd->lfd", selector, pieces, precision=lax.Precision.HIGHEST)
     return (d_gate, d_up, d_weight)

time: 567 us -> 608 us (1.072)
  local copies, waits for them, and re-layouts: 34.2 us -> 110 us
  waiting for transfers between devices: 459 us -> 417 us
  starting transfers between devices: 13.4 us -> 20.7 us
    split x0 -> x1, local copies, waits for them, and re-layouts: none -> 44.2 us  [shards(): jnp.split(partial_term.reshape(ff_dev, groups, feat_dev), lax.axis_size('...]
    all_to_all x1, waiting for transfers between devices: 44.2 us -> 0.01 us  [shards(): lax.all_to_all(slabs, 'dp', split_axis=0, concat_axis=2, tiled=True)]
    unnamed x15 -> x49, local copies, waits for them, and re-layouts: 7.12 us -> 49.5 us
    reshape x1 -> x0, local copies, waits for them, and re-layouts: 12 us -> none  [shards(): partial_term.reshape(ff_dev, groups, feat_dev)]
    all_to_all x1, starting transfers between devices: 5.16 us -> 12.6 us  [shards(): lax.all_to_all(jnp.stack(jnp.split(partial_term.reshape(ff_dev, groups, f...]
  transfers between devices with their start and end apart: 3 -> 3, of which waited for: 3 -> 2; matrix products, arithmetic and copies ran while one was open for 8% -> 22% of each run, Pallas kernels for 0% -> 0%
where the time goes in v1:
time: 608 us; the launch traced here: 607 us
  waiting for transfers between devices  417 us (69%)
  local copies, waits for them, and re-layouts  110 us (18%)
  matrix products  37.5 us (6%)
  starting transfers between devices  20.7 us (3%)
  between operations  14.2 us (2%)
  other arithmetic  7.66 us (1%)
    all_to_all x1, waiting for transfers between devices, shards(): lax.all_to_all(jnp.stack(jnp.split(partial_term.reshape(ff_dev, groups, f...  294 us
    all_gather x1, waiting for transfers between devices, shards(): out_rows = lax.all_gather(cotangent, 'tensor', axis=0, tiled=True)  122 us
    unnamed x49, local copies, waits for them, and re-layouts  49.5 us
    split x1, local copies, waits for them, and re-layouts, shards(): jnp.split(partial_term.reshape(ff_dev, groups, feat_dev), lax.axis_size('...  44.2 us
    dot_general x1, matrix products, shards(): jnp.einsum('lg,fgd->lfd', selector, pieces, precision=lax.Precision.HIGHEST)  18.1 us
    all_to_all x1, starting transfers between devices, shards(): lax.all_to_all(jnp.stack(jnp.split(partial_term.reshape(ff_dev, groups, f...  12.6 us
  transfers between devices with their start and end apart: 3, of which 2 were waited for; matrix products, arithmetic and copies ran while one was open for 22% of the time, Pallas kernels for 0%

profile of v1, /device:TPU:64, one launch (start us, length us, event | category | flops | bytes accessed | tf_op | source)
XLA Modules:
  0.0 606.6 jit_solution(5382738635096756557)
XLA Ops:
  7.2 0.7 all-gather.2.cloned.1.call-update
  8.7 4.0 gather_fusion
  12.7 7.0 %broadcast_select_fusion = bf16[16,896,256]{2,1,0:T(8,128)(2,1)} fusion(bf16[16,896,256]{2,1,0:T(8,128)(2,1)} %gather_fusion, pred[16]{0:T(512)(128)(4,1)S(1)} %compare_and_fusion), kind=kLoop, calls=%fused_computation.4 | loop fusion | flops 3670016 | bytes 14680080 | tf_op jit(solution)/shard_map/jit(_take)/select_n | solution.py:18
  19.7 8.0 %all-to-all-start = ((bf16[16,896,256]{2,1,0:T(8,128)(2,1)}), bf16[16,896,256]{2,1,0:T(8,128)(2,1)}, u32[]{:S(2)}, u32[]{:S(2)}) async-start(bf16[16,896,256]{2,1,0:T(8,128)(2,1)} %broadcast_select_fusion), calls=%async_computation | async-start | bytes 14680064 | tf_op jit(solution)/shard_map/all_to_all | solution.py:19
  28.9 122.2 %all-gather.2.cloned.1.call-done = bf16[512,4096]{1,0:T(8,128)(2,1)} async-done(((bf16[32,4096]{1,0:T(8,128)(2,1)}), bf16[512,4096]{1,0:T(8,128)(2,1)}) %all-gather.2.cloned.1.call-update) | async-done | bytes 4194320 | tf_op jit(solution)/shard_map/all_gather | solution.py:12
  151.0 9.6 %fusion.12 = f32[896,4096]{1,0:T(8,128)} fusion(bf16[512,4096]{1,0:T(8,128)(2,1)} %all-gather.2.cloned.1.call-done, bf16[512,896]{0,1:T(8,128)(2,1)S(1)} %copy.70, bf16[512,896]{0,1:T(8,128)(2,1)S(1)} %copy.71), kind=kOutput, calls=%fused_computation.20 | convolution fusion | flops 3761766400 | bytes 20709376 | tf_op jit(solution)/shard_map/dot_general | solution.py:29
  160.6 17.4 %copy.108 = f32[112,8,16,256]{3,2,1,0:T(8,128)} copy(f32[112,8,16,256]{3,1,2,0:T(8,128)} %bitcast.87) | data formatting | bytes 29360128
  178.0 44.2 %fusion.34 = (f32[896,1,256]{2,1,0:T(1,128)S(1)}, f32[896,1,256]{2,1,0:T(1,128)S(1)}, f32[896,1,256]{2,1,0:T(1,128)S(1)}, f32[896,1,256]{2,1,0:T(1,128)}, f32[89...) fusion(f32[896,16,256]{2,1,0:T(8,128)} %bitcast.86), kind=kLoop, calls=%fused_computation.60 | loop fusion | bytes 29360128 | tf_op jit(solution)/shard_map/split | solution.py:35
  222.3 2.3 fusion.29
  224.6 2.2 fusion.28
  226.8 2.2 fusion.27
  229.0 2.2 fusion.26
  231.2 2.2 fusion.25
  233.3 2.2 fusion.24
  235.5 2.3 fusion.23
  237.8 2.3 fusion.22
  240.0 1.0 fusion.21
  241.0 1.0 fusion.20
  242.0 1.0 fusion.19
  243.0 1.1 fusion.18
  244.1 1.0 fusion.17
  245.1 1.0 fusion.16
  246.1 1.0 fusion.15
  247.1 1.0 fusion.14
  248.1 12.6 %all-to-all-start.1 = ((f32[16,896,1,256]{3,1,2,0:T(8,128)}), f32[16,896,1,256]{3,1,2,0:T(8,128)}, u32[]{:S(2)}, u32[]{:S(2)}) async-start(f32[16,896,1,256]{3,1,2,0:T(8,128)} %fusion.14), calls=%async_computation.1 | async-start | bytes 29360128 | tf_op jit(solution)/shard_map/all_to_all | solution.py:33
  260.7 11.3 %copy.69 = bf16[1,896,16,256]{1,3,2,0:T(8,128)(2,1)} copy(bf16[1,896,16,256]{3,1,2,0:T(8,128)(2,1)} %bitcast.1) | data formatting | bytes 14680064 | tf_op jit(solution)/shard_map/all_to_all | solution.py:19
  272.0 9.8 %fusion.11 = (bf16[512,896]{0,1:T(8,128)(2,1)}, bf16[512,896]{0,1:T(8,128)(2,1)S(1)}) fusion(bf16[512,896]{0,1:T(8,128)(2,1)S(1)} %copy-done.10, bf16[512,896]{0,1:T(8,128)(2,1)S(1)} %copy-done.12, bf16[896,4096]{0,1:T(8,128)(2,1)} %bitcast.88, bf16[512,4096]{1,0:T(8,128)(2,1)} %all-gather.2.cloned.1.call-done), kind=kOutput, calls=%fused_computation.19 | convolution fusion | flops 3764977664 | bytes 15204352 | tf_op jit(solution)/shard_map/dot_general | solution.py:21
  281.8 2.3 copy.90
  284.1 1.3 copy.89
  285.4 293.7 %all-to-all-done.1 = f32[16,896,1,256]{3,1,2,0:T(8,128)} async-done(((f32[16,896,1,256]{3,1,2,0:T(8,128)}), f32[16,896,1,256]{3,1,2,0:T(8,128)}, u32[]{:S(2)}, u32[]{:S(2)}) %all-to-all-start.1) | async-done | bytes 14680096 | tf_op jit(solution)/shard_map/all_to_all | solution.py:33
  579.1 18.1 %fusion = f32[4,896,256]{2,0,1:T(4,128)S(1)} fusion(f32[16,896,1,256]{3,1,2,0:T(8,128)} %all-to-all-done.1, s32[16]{0:T(128)S(1)} %copy-done.13), kind=kOutput, calls=%fused_computation.1 | convolution fusion | flops 176160832 | bytes 18350144 | tf_op jit(solution)/shard_map/lg,fgd->lfd/dot_general | solution.py:45
  597.3 2.5 copy.91
  (35 shorter events, 1.9 us)
Async XLA Ops:
  7.2 1.5 copy-start
  7.2 5.5 copy-start.13
  7.2 143.8 %all-gather.2.cloned.1.call-start = ((), (), s32[]{:S(2)}) async-start(), calls=%async_computation.2 | async-start | bytes 4456448 | tf_op jit(solution)/shard_map/all_gather | solution.py:12
  12.7 15.0 %copy-start.7 = (bf16[512,896]{1,0:T(8,128)(2,1)S(1)}, bf16[512,896]{1,0:T(8,128)(2,1)}, u32[]{:S(2)}) copy-start(bf16[512,896]{1,0:T(8,128)(2,1)} %param.6) | copy-start | bytes 2752516
  12.7 15.6 %copy-start.8 = (bf16[512,896]{1,0:T(8,128)(2,1)S(1)}, bf16[512,896]{1,0:T(8,128)(2,1)}, u32[]{:S(2)}) copy-start(bf16[512,896]{1,0:T(8,128)(2,1)} %param.7) | copy-start | bytes 2752516
  19.7 228.4 %all-to-all-start = ((bf16[16,896,256]{2,1,0:T(8,128)(2,1)}), bf16[16,896,256]{2,1,0:T(8,128)(2,1)}, u32[]{:S(2)}, u32[]{:S(2)}) async-start(bf16[16,896,256]{2,1,0:T(8,128)(2,1)} %broadcast_select_fusion), calls=%async_computation | async-start | bytes 14680064 | tf_op jit(solution)/shard_map/all_to_all | solution.py:19
  28.3 149.7 %copy-start.9 = (bf16[512,896]{0,1:T(8,128)(2,1)}, bf16[512,896]{0,1:T(8,128)(2,1)S(1)}, u32[]{:S(2)}) copy-start(bf16[512,896]{0,1:T(8,128)(2,1)S(1)} %copy.71) | copy-start | bytes 2752516
  28.8 149.2 %copy-start.11 = (bf16[512,896]{0,1:T(8,128)(2,1)}, bf16[512,896]{0,1:T(8,128)(2,1)S(1)}, u32[]{:S(2)}) copy-start(bf16[512,896]{0,1:T(8,128)(2,1)S(1)} %copy.70) | copy-start | bytes 2752516
  222.2 17.8 %copy-start.6 = (f32[896,1,256]{2,1,0:T(1,128)S(1)}, f32[896,1,256]{2,1,0:T(1,128)}, u32[]{:S(2)}) copy-start(f32[896,1,256]{2,1,0:T(1,128)} %get-tuple-element.22) | copy-start | bytes 2752516
  222.2 18.8 %copy-start.5 = (f32[896,1,256]{2,1,0:T(1,128)S(1)}, f32[896,1,256]{2,1,0:T(1,128)}, u32[]{:S(2)}) copy-start(f32[896,1,256]{2,1,0:T(1,128)} %get-tuple-element.21) | copy-start | bytes 2752516
  222.3 19.7 %copy-start.4 = (f32[896,1,256]{2,1,0:T(1,128)S(1)}, f32[896,1,256]{2,1,0:T(1,128)}, u32[]{:S(2)}) copy-start(f32[896,1,256]{2,1,0:T(1,128)} %get-tuple-element.20) | copy-start | bytes 2752516
  222.3 20.7 %copy-start.3 = (f32[896,1,256]{2,1,0:T(1,128)S(1)}, f32[896,1,256]{2,1,0:T(1,128)}, u32[]{:S(2)}) copy-start(f32[896,1,256]{2,1,0:T(1,128)} %get-tuple-element.19) | copy-start | bytes 2752516
  222.3 21.8 %copy-start.2 = (f32[896,1,256]{2,1,0:T(1,128)S(1)}, f32[896,1,256]{2,1,0:T(1,128)}, u32[]{:S(2)}) copy-start(f32[896,1,256]{2,1,0:T(1,128)} %get-tuple-element.18) | copy-start | bytes 2752516
  248.1 331.0 %all-to-all-start.1 = ((f32[16,896,1,256]{3,1,2,0:T(8,128)}), f32[16,896,1,256]{3,1,2,0:T(8,128)}, u32[]{:S(2)}, u32[]{:S(2)}) async-start(f32[16,896,1,256]{3,1,2,0:T(8,128)} %fusion.14), calls=%async_computation.1 | async-start | bytes 29360128 | tf_op jit(solution)/shard_map/all_to_all | solution.py:33
  260.7 11.3 %copy-start.10 = (bf16[512,896]{0,1:T(8,128)(2,1)S(1)}, bf16[512,896]{0,1:T(8,128)(2,1)}, u32[]{:S(2)}) copy-start(bf16[512,896]{0,1:T(8,128)(2,1)} %copy-done.9) | copy-start | bytes 2752516
  260.7 11.3 %copy-start.12 = (bf16[512,896]{0,1:T(8,128)(2,1)S(1)}, bf16[512,896]{0,1:T(8,128)(2,1)}, u32[]{:S(2)}) copy-start(bf16[512,896]{0,1:T(8,128)(2,1)} %copy-done.11) | copy-start | bytes 2752516
  281.8 318.0 %copy-start.1 = (bf16[4,896,256]{2,1,0:T(8,128)(2,1)S(1)}, bf16[4,896,256]{2,1,0:T(8,128)(2,1)}, u32[]{:S(2)}) copy-start(bf16[4,896,256]{2,1,0:T(8,128)(2,1)} %param.8) | copy-start | bytes 5505028
Sparse Core Ops, SparseCore 0:
  10.8 140.2 all-gather.1
